TPU v7x, 128 devices: a whole 4x4x4 slice. The times are simulated.
128 devices in a mesh: wave: 8 (over z_lo, x), strip: 16 (over y, z_hi, core).
Axes of the slice: x: 4, y: 4, z: 4 (z_hi: 2, z_lo: 2; z = z_hi * 2 + z_lo), core: 2. Of those that a mesh axis runs over, the one named last changes fastest.
Arguments:
- unit_params: float32 [9, 16, 24576], P(None, 'strip', 'wave'), may hold values from 0 to 1
- observed: bfloat16 [4, 256, 1536, 256], P(None, 'wave', 'strip'), may hold values from -3 to 3
- psf_rows: bfloat16 [256, 4, 65], P('wave'), may hold values from -0.75 to 0.75
- psf_cols: bfloat16 [256, 4, 65], P('wave'), may hold values from -0.75 to 0.75
- pixel_mask: int32 [1536, 256], P('strip'), may hold values 0 or 1
- strip_lengths: int32 [16], P('strip'), may hold values from 32 to 96, as said below
Outputs:
- param_grad: float32 [9, 16, 24576], P(None, 'strip', 'wave')
Inputs may be any that keep to these rules, and one draw needn't show every extreme that they name: `strip_lengths`: the strip lengths sum to 1024; in every draw one strip holds 96 rows and one holds 32.
All inputs are finite; a program needn't handle non-finite values. No bound on the sum of `pixel_mask` on one device may be relied on, other than what follows from the above.
Results may differ from a plain program's by a relative error of at most 0.00098.
Values may be sent and summed in bfloat16 or wider, within the bound.
No kernel may reach another device: no remote copies, remote signals or barrier semaphores. Data moves between devices by JAX's collectives and lax.ppermute only.
A program may use at most 192 MiB of HBM per device.

v0:
```python
import jax
import jax.numpy as jnp
from jax import lax
from jax.sharding import PartitionSpec as P

parameter_low = (0.2, 0.4, 2.0, -0.8, 0.4, 0.3, 0.0, 0.0, 0.0)
parameter_span = (0.4, 0.6, 18.0, 1.6, 0.8, 1.2, 1.5, 3.141592653589793, 3.141592653589793)
stokes_weight = (1.0, 3.0, 3.0, 2.0)
loss_scale = 0.03125


def passed_along(shard, axis, by):
    count = lax.axis_size(axis)
    pairs = [(i, i + by) for i in range(count) if 0 <= i + by < count]
    return lax.ppermute(shard, axis, pairs)


def profile(distance, damping):
    scaled = distance / damping
    return 1.0 / (1.0 + scaled * scaled)


def stokes_model(unit_params, wave_grid):
    physical = [
        parameter_low[number] + parameter_span[number] * unit_params[number] for number in range(9)
    ]
    (
        source_zero,
        source_slope,
        strength,
        doppler,
        line_width,
        damping,
        zeeman_split,
        incline,
        azimuth,
    ) = physical
    offset = (wave_grid[:, None, None] - doppler) / line_width
    split_ratio = zeeman_split / line_width
    centre = profile(offset, damping)
    upper_line = profile(offset - split_ratio, damping)
    lower_line = profile(offset + split_ratio, damping)
    cosine = jnp.cos(incline)
    sine_value = jnp.sin(incline)
    sine_square = sine_value * sine_value
    absorb_total = 1.0 + strength * (
        centre * sine_square * 0.5 + (upper_line + lower_line) * (1.0 + cosine * cosine) * 0.25
    )
    linear = strength * (centre - 0.5 * (upper_line + lower_line)) * sine_square * 0.5
    linear_cosine = linear * jnp.cos(2.0 * azimuth)
    linear_sine = linear * jnp.sin(2.0 * azimuth)
    circular = strength * (lower_line - upper_line) * cosine * 0.5
    denominator = (
        absorb_total * absorb_total
        - linear_cosine * linear_cosine
        - linear_sine * linear_sine
        - circular * circular
    )
    source_ratio = source_slope / denominator
    return jnp.stack(
        [
            source_zero + source_ratio * absorb_total,
            -source_ratio * linear_cosine,
            -source_ratio * linear_sine,
            -source_ratio * circular,
        ]
    )


def band_tables(tap_table, out_rows, tap_count):
    in_rows = out_rows + tap_count - 1
    target_row = lax.broadcasted_iota(jnp.int32, (out_rows, in_rows, tap_count), 0)
    source_row = lax.broadcasted_iota(jnp.int32, (out_rows, in_rows, tap_count), 1)
    tap_index = lax.broadcasted_iota(jnp.int32, (out_rows, in_rows, tap_count), 2)
    selector = (source_row - target_row == tap_index).astype(jnp.bfloat16)
    return jnp.einsum(
        "wkt,ijt->wkij", tap_table, selector, preferred_element_type=jnp.float32
    ).astype(jnp.bfloat16)


def column_tables(tap_table, columns, tap_count):
    radius = tap_count // 2
    source_column = lax.broadcasted_iota(jnp.int32, (columns, columns, tap_count), 0)
    target_column = lax.broadcasted_iota(jnp.int32, (columns, columns, tap_count), 1)
    tap_index = lax.broadcasted_iota(jnp.int32, (columns, columns, tap_count), 2)
    selector = (source_column - target_column + radius == tap_index).astype(jnp.bfloat16)
    return jnp.einsum(
        "wkt,xyt->wkxy", tap_table, selector, preferred_element_type=jnp.float32
    ).astype(jnp.bfloat16)


def extend(upper_rim, middle, lower_rim, length, axis_index):
    radius = upper_rim.shape[axis_index]
    widened = jnp.concatenate([upper_rim, middle, jnp.zeros_like(upper_rim)], axis=axis_index)
    return lax.dynamic_update_slice_in_dim(widened, lower_rim, radius + length, axis_index)


def per_device(unit_params, observed, psf_rows, psf_cols, pixel_mask, strip_lengths):
    stokes_count, wave_count, capacity, columns = observed.shape
    tap_count = psf_rows.shape[2]
    radius = tap_count // 2
    gathered = lax.all_gather(unit_params, "wave", axis=2, tiled=True)
    own_params = gathered.reshape(gathered.shape[0], capacity, columns)
    length = strip_lengths[0]
    wave_pos = lax.axis_index("wave")
    levels = (wave_pos * wave_count + jnp.arange(wave_count, dtype=jnp.int32)).astype(jnp.float32)
    wave_grid = -3.0 + 6.0 * levels / (wave_count * lax.axis_size("wave") - 1)
    row_index = jnp.arange(capacity, dtype=jnp.int32)
    rows_live = (row_index < length).astype(jnp.float32)
    model_own = (stokes_model(own_params, wave_grid) * rows_live[:, None]).astype(jnp.bfloat16)
    tail_rows = lax.dynamic_slice_in_dim(model_own, length - radius, radius, 2)
    upper_rim = passed_along(tail_rows, "strip", 1)
    lower_rim = passed_along(model_own[:, :, :radius], "strip", -1)
    model_wide = extend(upper_rim, model_own, lower_rim, length, 2)
    row_band = band_tables(psf_rows, capacity, tap_count)
    column_band = column_tables(psf_cols, columns, tap_count)
    live_mask = pixel_mask.astype(jnp.float32) * rows_live[:, None]
    weight_square = jnp.array(stokes_weight, jnp.float32)
    weight_square = weight_square * weight_square
    block_size = 4
    block_count = wave_count // block_size

    def forward(number, residual_all):
        first_wave = number * block_size
        model_block = lax.dynamic_slice_in_dim(model_wide, first_wave, block_size, 1)
        band_block = lax.dynamic_slice_in_dim(row_band, first_wave, block_size, 0)
        column_block = lax.dynamic_slice_in_dim(column_band, first_wave, block_size, 0)
        observed_block = lax.dynamic_slice_in_dim(observed, first_wave, block_size, 1)
        row_pass = jnp.einsum(
            "wkij,swjc->kswic", band_block, model_block, preferred_element_type=jnp.float32
        ).astype(jnp.bfloat16)
        blurred = jnp.einsum(
            "kswic,wkcd->swid", row_pass, column_block, preferred_element_type=jnp.float32
        )
        residual = (
            loss_scale
            * weight_square[:, None, None, None]
            * live_mask
            * (blurred - observed_block.astype(jnp.float32))
        ).astype(jnp.bfloat16)
        return lax.dynamic_update_slice_in_dim(residual_all, residual, first_wave, 1)

    residual_all = lax.fori_loop(0, block_count, forward, jnp.zeros(observed.shape, jnp.bfloat16))
    row_back = band_tables(psf_rows[:, :, ::-1], capacity, tap_count)
    tail_residual = lax.dynamic_slice_in_dim(residual_all, length - radius, radius, 2)
    upper_resid = passed_along(tail_residual, "strip", 1)
    lower_resid = passed_along(residual_all[:, :, :radius], "strip", -1)
    residual_wide = extend(upper_resid, residual_all, lower_resid, length, 2)

    def backward(number, gradient_sum):
        first_wave = number * block_size
        residual_block = lax.dynamic_slice_in_dim(residual_wide, first_wave, block_size, 1)
        column_block = lax.dynamic_slice_in_dim(column_band, first_wave, block_size, 0)
        back_block = lax.dynamic_slice_in_dim(row_back, first_wave, block_size, 0)
        grid_block = lax.dynamic_slice_in_dim(wave_grid, first_wave, block_size, 0)
        across = jnp.einsum(
            "swjc,wkdc->kswjd", residual_block, column_block, preferred_element_type=jnp.float32
        ).astype(jnp.bfloat16)
        adjoint = (
            jnp.einsum("wkij,kswjc->swic", back_block, across, preferred_element_type=jnp.float32)
            * rows_live[:, None]
        )

        def model_of(params_now):
            return stokes_model(params_now, grid_block)

        unused_model, pullback = jax.vjp(model_of, own_params)
        return gradient_sum + pullback(adjoint)[0]

    gradient_local = lax.fori_loop(
        0, block_count, backward, jnp.zeros(own_params.shape, jnp.float32)
    )
    gradient_flat = gradient_local.reshape(gathered.shape)
    gradient_total = lax.psum(gradient_flat, "wave")
    share_width = unit_params.shape[2]
    return lax.dynamic_slice_in_dim(gradient_total, wave_pos * share_width, share_width, 2)


def solution(mesh):
    return jax.shard_map(
        per_device,
        mesh=mesh,
        in_specs=(
            P(None, "strip", "wave"),
            P(None, "wave", "strip", None),
            P("wave", None, None),
            P("wave", None, None),
            P("strip", None),
            P("strip"),
        ),
        out_specs=P(None, "strip", "wave"),
        check_vma=False,
    )
```

profile of v0, /device:TPU:0, one launch (start us, length us, event | category | flops | bytes accessed | tf_op | source)
XLA Modules:
  0.0 510.9 jit_solution(6636742498582574275)
XLA Ops:
  6.5 31.1 %all_gather.3 = f32[9,1,24576]{2,1,0:T(1,128)S(1)} all-gather(f32[9,1,3072]{2,1,0:T(1,128)} %param.11), channel_id=1, replica_groups=mesh['wave'=8,'strip'=16] {'wave'}, dimensions={2}, use_global_device_ids=true | all-gather | bytes 995328 | tf_op jit(solution)/shard_map/all_gather | solution.py:102
  37.6 9.9 %fusion.103 = (f32[24576]{0:T(1024)S(1)}, f32[24576]{0:T(1024)S(1)}, f32[24576]{0:T(1024)S(1)}, f32[24576]{0:T(1024)S(1)}, f32[24576]{0:T(1024)S(1)}, /*index=5*...) fusion(f32[9,1,24576]{2,1,0:T(1,128)S(1)} %all_gather.3), kind=kLoop, calls=%fused_computation.198 | loop fusion | flops 442368 | bytes 1966080 | tf_op jit(solution)/shard_map/add | solution.py:25
  48.7 5.3 %multiply_add_fusion.8 = (f32[1,32,96,256]{3,2,1,0:T(8,128)S(1)}, f32[1,32,96,256]{3,2,1,0:T(8,128)S(1)}, f32[1,32,96,256]{3,2,1,0:T(8,128)S(1)}, f32[1,32,96,256]{3,2,1,0:T(8,128)S(1)}) fusion(f32[96,256]{1,0:T(8,128)S(1)} %get-tuple-element.546, f32[96,256]{1,0:T(8,128)S(1)} %add.585, f32[96,256]{1,0:T(8,128)S(1)} %get-tuple-element.545, ...), kind=kLoop, calls=%fused_computation.166 | loop fusion | flops 37748736 | bytes 13860992 | tf_op jit(solution)/shard_map/add | solution.py:62
  54.0 2.0 fusion.74
  56.1 3.7 fusion.113
  60.0 2.6 collective-permute-start
  64.1 8.5 %convert_bitcast_fusion = bf16[32,4,256,256]{3,0,1,2:T(8,128)(2,1)} fusion(bf16[32,4,65]{2,1,0:T(4,128)(2,1)S(1)} %copy-done.4), kind=kOutput, calls=%fused_computation.149 | convolution fusion | flops 1111687168 | bytes 16793856 | tf_op jit(solution)/shard_map/wkt,xyt->wkxy/dot_general | solution.py:87
  72.6 16.3 %copy.20 = bf16[32,4,256,256]{3,2,1,0:T(8,128)(2,1)} copy(bf16[32,4,256,256]{3,0,1,2:T(8,128)(2,1)} %convert_bitcast_fusion) | data formatting | bytes 33554432
  89.0 3.9 convert_bitcast_fusion.2
  92.9 10.1 %maximum_maximum_fusion = bf16[4,32,160,256]{3,2,1,0:T(8,128)(2,1)} fusion(bf16[4,32,96,256]{3,2,1,0:T(8,128)(2,1)} %copy-done.1, bf16[4,32,32,256]{3,2,1,0:T(8,128)(2,1)} %collective-permute-done, bf16[160]{0:T(256)(128)(2,1)S(1)} %pad.113.clone), kind=kLoop, calls=%fused_computation.152 | loop fusion | flops 31457280 | bytes 18874688 | tf_op jit(solution)/shard_map/concatenate | solution.py:94
  103.0 20.4 %dynamic_update_slice.13 = bf16[4,32,160,256]{3,2,1,0:T(8,128)(2,1)} dynamic-update-slice(bf16[4,32,160,256]{3,2,1,0:T(8,128)(2,1)} %maximum_maximum_fusion, bf16[4,32,32,256]{3,2,1,0:T(8,128)(2,1)} %collective-permute-done.1, s32[]{:T(128)} %constant.278.clone.1, s32[]{:T(128)} %constant.278.clone.1, s32[]{:T(128)S(6)} %select_n.37, s32[]{:T(128)} %constant.278.clone.1) | dynamic-update-slice | bytes 4194308 | tf_op jit(solution)/shard_map/dynamic_update_slice | solution.py:95
  123.3 3.4 broadcast_in_dim.105.clone
  126.7 58.5 %while.31 = (s32[]{:T(128)}, bf16[4,32,96,256]{3,2,1,0:T(8,128)(2,1)}, f32[96,256]{1,0:T(8,128)S(1)}, bf16[32,4,256,256]{3,2,1,0:T(8,128)(2,1)}, bf16[4,32,160,2...) while((s32[]{:T(128)}, ...), condition=%wide.region_1.0_spmd.clone, body=%wide.region_0.0_spmd.clone.sunk | while | flops 1311866880 | bytes 9897691 | solution.py:143
  126.7 1.7 constant_dynamic-slice_fusion.11
  129.1 4.0 fusion.130
  134.0 1.7 constant_dynamic-slice_fusion.11
  136.4 4.0 fusion.130
  141.3 1.7 constant_dynamic-slice_fusion.11
  143.7 4.0 fusion.130
  148.6 1.7 constant_dynamic-slice_fusion.11
  151.0 4.0 fusion.130
  155.9 1.7 constant_dynamic-slice_fusion.11
  158.3 4.0 fusion.130
  163.2 1.7 constant_dynamic-slice_fusion.11
  165.6 4.0 fusion.130
  170.6 1.7 constant_dynamic-slice_fusion.11
  173.0 4.0 fusion.130
  177.9 1.7 constant_dynamic-slice_fusion.11
  180.3 4.0 fusion.130
  185.2 5.4 %fusion.112 = (bf16[4,32,32,256]{3,2,1,0:T(8,128)(2,1)}, bf16[4,32,32,256]{3,2,1,0:T(8,128)(2,1)}) fusion(bf16[4,32,96,256]{3,2,1,0:T(8,128)(2,1)} %get-tuple-element.364, s32[]{:T(128)S(6)} %select_n.36), kind=kLoop, calls=%fused_computation.217 | loop fusion | bytes 8388612 | tf_op jit(solution)/shard_map/slice | solution.py:147
  190.6 22.0 %collective-permute-start.2 = (bf16[4,32,32,256]{3,2,1,0:T(8,128)(2,1)}, bf16[4,32,32,256]{3,2,1,0:T(8,128)(2,1)}, u32[]{:S(2)}, u32[]{:S(2)}) collective-permute-start(bf16[4,32,32,256]{3,2,1,0:T(8,128)(2,1)} %get-tuple-element.537), channel_id=1, source_target_pairs={{0,1},{1,2},{2,3},{3,4},{4,5},{5,6},{6,7},{7,8},{8,9},{9,10},{10,1... | collective-permute-start | bytes 6291464 | tf_op jit(solution)/shard_map/ppermute | solution.py:15
  212.6 1.5 collective-permute-start.3
  214.2 3.6 reduce.1
  217.8 1.9 copy.40
  219.7 4.0 convert_bitcast_fusion.1
  223.7 7.9 %maximum_maximum_fusion.1 = bf16[4,32,160,256]{3,2,1,0:T(8,128)(2,1)} fusion(bf16[4,32,96,256]{3,2,1,0:T(8,128)(2,1)S(1)} %copy-done, bf16[4,32,32,256]{3,2,1,0:T(8,128)(2,1)} %collective-permute-done.2, bf16[160]{0:T(256)(128)(2,1)S(1)} %pad.113.clone), kind=kLoop, calls=%fused_computation.153 | loop fusion | flops 31457280 | bytes 18874688 | tf_op jit(solution)/shard_map/concatenate | solution.py:94
  231.6 20.4 %dynamic_update_slice.14 = bf16[4,32,160,256]{3,2,1,0:T(8,128)(2,1)} dynamic-update-slice(bf16[4,32,160,256]{3,2,1,0:T(8,128)(2,1)} %maximum_maximum_fusion.1, bf16[4,32,32,256]{3,2,1,0:T(8,128)(2,1)} %collective-permute-done.3, s32[]{:T(128)} %constant.278.clone.1, s32[]{:T(128)} %constant.278.clone.1, s32[]{:T(128)S(6)} %select_n.37, s32[]{:T(128)} %constant.278.clone.1) | dynamic-update-slice | bytes 4194308 | tf_op jit(solution)/shard_map/dynamic_update_slice | solution.py:95
  252.0 134.8 %while.32 = (s32[]{:T(128)}, f32[9,96,256]{2,1,0:T(8,128)S(1)}, f32[9,96,256]{2,1,0:T(8,128)S(1)}, f32[32]{0:T(128)S(1)}, bf16[32,4,256,256]{3,2,1,0:T(8,128)(2,...) while((s32[]{:T(128)}, f32[9,96,256]{2,1,0:T(8,128)S(1)}, ...), condition=%wide.region_21.22_spmd.clone, body=%wide.region_2.21_spmd.clone.sunk | while | flops 1872642304 | bytes 34342920 | solution.py:170
  252.0 2.5 constant_dynamic-slice_fusion.12
  255.2 4.9 fusion.134
  265.2 1.5 fusion.136
  268.8 2.5 constant_dynamic-slice_fusion.12
  272.0 4.9 fusion.134
  282.0 1.5 fusion.136
  285.7 2.5 constant_dynamic-slice_fusion.12
  288.9 4.9 fusion.134
  298.9 1.5 fusion.136
  302.5 2.5 constant_dynamic-slice_fusion.12
  305.7 4.9 fusion.134
  315.7 1.5 fusion.136
  319.4 2.5 constant_dynamic-slice_fusion.12
  322.6 4.9 fusion.134
  332.6 1.5 fusion.136
  336.2 2.5 constant_dynamic-slice_fusion.12
  339.4 4.9 fusion.134
  349.5 1.5 fusion.136
  353.1 2.5 constant_dynamic-slice_fusion.12
  356.3 4.9 fusion.134
  366.3 1.5 fusion.136
  369.9 2.5 constant_dynamic-slice_fusion.12
  373.1 4.9 fusion.134
  386.8 1.8 reshape.646
  388.6 113.9 %all-reduce.11.cloned.1.call-done = f32[9,1,24576]{2,1,0:T(1,128)} async-done(((f32[9,1,24576]{2,1,0:T(1,128)}), f32[9,1,24576]{2,1,0:T(1,128)}) %all-reduce.11.cloned.1.call-update) | async-done | bytes 884752 | tf_op jit(solution)/shard_map/psum | solution.py:174
  502.5 1.5 constant_dynamic-slice_fusion.3
  (176 shorter events, 80.4 us)
Async XLA Ops:
  6.5 496.0 %all-reduce.11.cloned.1.call-start = ((), (), s32[]{:S(2)}) async-start(), calls=%async_computation | async-start | bytes 1769472 | tf_op jit(solution)/shard_map/psum | solution.py:174
  56.1 3.9 copy-start.1
  56.1 8.0 %copy-start.4 = (bf16[32,4,65]{2,1,0:T(4,128)(2,1)S(1)}, bf16[32,4,65]{2,1,0:T(4,128)(2,1)}, u32[]{:S(2)}) copy-start(bf16[32,4,65]{2,1,0:T(4,128)(2,1)} %param.14) | copy-start | bytes 49924
  60.0 32.9 %collective-permute-start = (bf16[4,32,32,256]{3,2,1,0:T(8,128)(2,1)}, bf16[4,32,32,256]{3,2,1,0:T(8,128)(2,1)}, u32[]{:S(2)}, u32[]{:S(2)}) collective-permute-start(bf16[4,32,32,256]{3,2,1,0:T(8,128)(2,1)} %get-tuple-element.539), channel_id=1, source_target_pairs={{0,1},{1,2},{2,3},{3,4},{4,5},{5,6},{6,7},{7,8},{8,9},{9,10},{10,1... | collective-permute-start | bytes 6291464 | tf_op jit(solution)/shard_map/ppermute | solution.py:15
  62.6 40.3 %collective-permute-start.1 = (bf16[4,32,32,256]{3,2,1,0:T(8,128)(2,1)}, bf16[4,32,32,256]{3,2,1,0:T(8,128)(2,1)}, u32[]{:S(2)}, u32[]{:S(2)}) collective-permute-start(bf16[4,32,32,256]{3,2,1,0:T(8,128)(2,1)} %get-tuple-element.538), channel_id=1, source_target_pairs={{1,0},{2,1},{3,2},{4,3},{5,4},{6,5},{7,6},{8,7},{9,8},{10,9},{11,1... | collective-permute-start | bytes 6291464 | tf_op jit(solution)/shard_map/ppermute | solution.py:15
  72.6 16.4 %copy-start.3 = (s32[96,256]{1,0:T(8,128)S(1)}, s32[96,256]{1,0:T(8,128)}, u32[]{:S(2)}) copy-start(s32[96,256]{1,0:T(8,128)} %param.15) | copy-start | bytes 294916
  72.6 16.4 %copy-start.2 = (bf16[32,4,65]{2,1,0:T(4,128)(2,1)S(1)}, bf16[32,4,65]{2,1,0:T(4,128)(2,1)}, u32[]{:S(2)}) copy-start(bf16[32,4,65]{2,1,0:T(4,128)(2,1)} %param.13) | copy-start | bytes 49924
  123.3 3.4 copy-start.5
  190.6 33.1 %collective-permute-start.2 = (bf16[4,32,32,256]{3,2,1,0:T(8,128)(2,1)}, bf16[4,32,32,256]{3,2,1,0:T(8,128)(2,1)}, u32[]{:S(2)}, u32[]{:S(2)}) collective-permute-start(bf16[4,32,32,256]{3,2,1,0:T(8,128)(2,1)} %get-tuple-element.537), channel_id=1, source_target_pairs={{0,1},{1,2},{2,3},{3,4},{4,5},{5,6},{6,7},{7,8},{8,9},{9,10},{10,1... | collective-permute-start | bytes 6291464 | tf_op jit(solution)/shard_map/ppermute | solution.py:15
  212.6 19.0 %collective-permute-start.3 = (bf16[4,32,32,256]{3,2,1,0:T(8,128)(2,1)}, bf16[4,32,32,256]{3,2,1,0:T(8,128)(2,1)}, u32[]{:S(2)}, u32[]{:S(2)}) collective-permute-start(bf16[4,32,32,256]{3,2,1,0:T(8,128)(2,1)} %get-tuple-element.536), channel_id=1, source_target_pairs={{1,0},{2,1},{3,2},{4,3},{5,4},{6,5},{7,6},{8,7},{9,8},{10,9},{11,1... | collective-permute-start | bytes 6291464 | tf_op jit(solution)/shard_map/ppermute | solution.py:15
  219.7 4.0 copy-start
Sparse Core Ops, SparseCore 0:
  388.8 113.6 all-reduce.10
where the time goes:
time: 514 us; the launch traced here: 511 us
  local copies, waits for them, and re-layouts  122 us (24%)
  other arithmetic  114 us (22%)
  waiting for transfers between devices  114 us (22%)
  matrix products  87 us (17%)
  blocking collectives  31.1 us (6%)
  starting transfers between devices  27.5 us (5%)
  between operations  14.3 us (3%)
    psum x1, waiting for transfers between devices, per_device(): gradient_total = lax.psum(gradient_flat, 'wave')  114 us
    dynamic_update_slice x2, local copies, waits for them, and re-layouts, extend(): lax.dynamic_update_slice_in_dim(widened, lower_rim, radius + length, axis...  40.8 us
    dot_general x8, matrix products, backward(): jnp.einsum('wkij,kswjc->swic', back_block, across, preferred_element_type...  39.1 us
    dot_general x8, matrix products, forward(): jnp.einsum('kswic,wkcd->swid', row_pass, column_block, preferred_element_...  31.6 us
    all_gather x1, blocking collectives, per_device(): gathered = lax.all_gather(unit_params, 'wave', axis=2, tiled=True)  31.1 us
    ppermute x4, starting transfers between devices, passed_along(): return lax.ppermute(shard, axis, pairs)  27.5 us
    mul x32, other arithmetic, stokes_model(): parameter_span[number] * unit_params[number]  22.7 us
    dynamic_slice x8, local copies, waits for them, and re-layouts, backward(): back_block = lax.dynamic_slice_in_dim(row_back, first_wave, block_size, 0)  20.2 us
  transfers between devices with their start and end apart: 5, of which 1 were waited for; matrix products, arithmetic and copies ran while one was open for 11% of the time, Pallas kernels for 0%

commit v1 on v0

--- a/solution.py
+++ b/solution.py
@@ -7,6 +7,12 @@
 parameter_span = (0.4, 0.6, 18.0, 1.6, 0.8, 1.2, 1.5, 3.141592653589793, 3.141592653589793)
 stokes_weight = (1.0, 3.0, 3.0, 2.0)
 loss_scale = 0.03125
+
+
+def summed_here(array, mesh_axis):
+    parts = lax.all_gather(array, mesh_axis, axis=0, tiled=False)
+    total = parts.sum(axis=0)
+    return total
 
 
 def passed_along(shard, axis, by):
@@ -171,7 +177,7 @@
         0, block_count, backward, jnp.zeros(own_params.shape, jnp.float32)
     )
     gradient_flat = gradient_local.reshape(gathered.shape)
-    gradient_total = lax.psum(gradient_flat, "wave")
+    gradient_total = summed_here(gradient_flat, "wave")
     share_width = unit_params.shape[2]
     return lax.dynamic_slice_in_dim(gradient_total, wave_pos * share_width, share_width, 2)
 

time: 514 us -> 531 us (1.033)
  other arithmetic: 114 us -> 133 us
  local copies, waits for them, and re-layouts: 122 us -> 107 us
  matrix products: 87 us -> 94.7 us
  waiting for transfers between devices: 114 us -> 120 us
    all_gather x0 -> x1, waiting for transfers between devices: none -> 120 us  [summed_here(): parts = lax.all_gather(array, mesh_axis, axis=0, tiled=False)]
    psum x1 -> x0, waiting for transfers between devices: 114 us -> none  [per_device(): gradient_total = lax.psum(gradient_flat, 'wave')]
    reduce_sum x0 -> x1, other arithmetic: none -> 19.7 us  [summed_here(): total = parts.sum(axis=0)]
    dot_general x8, matrix products: 31.6 us -> 39.3 us  [forward(): jnp.einsum('kswic,wkcd->swid', row_pass, column_block, preferred_element_...]
    dynamic_update_slice x8 -> x0, local copies, waits for them, and re-layouts: 7.64 us -> none  [forward(): lax.dynamic_update_slice_in_dim(residual_all, residual, first_wave, 1)]
    dynamic_slice x16 -> x8, local copies, waits for them, and re-layouts: 18.2 us -> 13.3 us  [forward(): band_block = lax.dynamic_slice_in_dim(row_band, first_wave, block_size, 0)]
  transfers between devices with their start and end apart: 5 -> 5, of which waited for: 1 -> 1; matrix products, arithmetic and copies ran while one was open for 11% -> 10% of each run, Pallas kernels for 0% -> 0%
where the time goes in v1:
time: 531 us; the launch traced here: 528 us
  other arithmetic  133 us (25%)
  waiting for transfers between devices  120 us (23%)
  local copies, waits for them, and re-layouts  107 us (20%)
  matrix products  94.7 us (18%)
  blocking collectives  31.1 us (6%)
  starting transfers between devices  27.4 us (5%)
  between operations  14.3 us (3%)
    all_gather x1, waiting for transfers between devices, summed_here(): parts = lax.all_gather(array, mesh_axis, axis=0, tiled=False)  120 us
    dynamic_update_slice x2, local copies, waits for them, and re-layouts, extend(): lax.dynamic_update_slice_in_dim(widened, lower_rim, radius + length, axis...  40.4 us
    dot_general x8, matrix products, forward(): jnp.einsum('kswic,wkcd->swid', row_pass, column_block, preferred_element_...  39.3 us
    dot_general x8, matrix products, backward(): jnp.einsum('wkij,kswjc->swic', back_block, across, preferred_element_type...  39 us
    all_gather x1, blocking collectives, per_device(): gathered = lax.all_gather(unit_params, 'wave', axis=2, tiled=True)  31.1 us
    ppermute x4, starting transfers between devices, passed_along(): return lax.ppermute(shard, axis, pairs)  27.3 us
    mul x32, other arithmetic, stokes_model(): parameter_span[number] * unit_params[number]  22.7 us
    dynamic_slice x8, local copies, waits for them, and re-layouts, backward(): back_block = lax.dynamic_slice_in_dim(row_back, first_wave, block_size, 0)  20.2 us
  transfers between devices with their start and end apart: 5, of which 1 were waited for; matrix products, arithmetic and copies ran while one was open for 10% of the time, Pallas kernels for 0%

profile of v1, /device:TPU:0, one launch (start us, length us, event | category | flops | bytes accessed | tf_op | source)
XLA Modules:
  0.0 527.6 jit_solution(13017271283852919784)
XLA Ops:
  6.5 31.1 %all_gather.6 = f32[9,1,24576]{2,1,0:T(1,128)S(1)} all-gather(f32[9,1,3072]{2,1,0:T(1,128)} %param.11), channel_id=1, replica_groups=mesh['wave'=8,'strip'=16] {'wave'}, dimensions={2}, use_global_device_ids=true | all-gather | bytes 995328 | tf_op jit(solution)/shard_map/all_gather | solution.py:108
  37.6 9.9 %fusion.111 = (f32[24576]{0:T(1024)S(1)}, f32[24576]{0:T(1024)S(1)}, f32[24576]{0:T(1024)S(1)}, f32[24576]{0:T(1024)S(1)}, f32[24576]{0:T(1024)S(1)}, /*index=5*...) fusion(f32[9,1,24576]{2,1,0:T(1,128)S(1)} %all_gather.6), kind=kLoop, calls=%fused_computation.198 | loop fusion | flops 442368 | bytes 1966080 | tf_op jit(solution)/shard_map/add | solution.py:31
  48.7 5.3 %multiply_add_fusion.8 = (f32[1,32,96,256]{3,2,0,1:T(8,128)S(1)}, f32[1,32,96,256]{3,2,0,1:T(8,128)S(1)}, f32[1,32,96,256]{3,2,0,1:T(8,128)S(1)}, f32[1,32,96,256]{3,2,0,1:T(8,128)S(1)}) fusion(f32[96,256]{1,0:T(8,128)S(1)} %get-tuple-element.576, f32[96,256]{1,0:T(8,128)S(1)} %add.583, f32[96,256]{1,0:T(8,128)S(1)} %get-tuple-element.575, ...), kind=kLoop, calls=%fused_computation.166 | loop fusion | flops 37748736 | bytes 13860992 | tf_op jit(solution)/shard_map/add | solution.py:68
  54.0 2.1 fusion.82
  56.1 3.7 fusion.121
  60.0 2.6 collective-permute-start
  62.7 1.5 collective-permute-start.1
  64.1 8.5 %convert_bitcast_fusion = bf16[32,4,256,256]{3,0,1,2:T(8,128)(2,1)} fusion(bf16[32,4,65]{2,1,0:T(4,128)(2,1)S(1)} %copy-done.4), kind=kOutput, calls=%fused_computation.149 | convolution fusion | flops 1111687168 | bytes 16793856 | tf_op jit(solution)/shard_map/wkt,xyt->wkxy/dot_general | solution.py:93
  72.6 16.3 %copy.45 = bf16[32,4,256,256]{3,2,1,0:T(8,128)(2,1)} copy(bf16[32,4,256,256]{3,0,1,2:T(8,128)(2,1)} %convert_bitcast_fusion) | data formatting | bytes 33554432
  89.1 3.9 convert_bitcast_fusion.2
  92.9 10.1 %maximum_maximum_fusion = bf16[4,32,160,256]{3,2,0,1:T(8,128)(2,1)} fusion(bf16[4,32,96,256]{3,2,0,1:T(8,128)(2,1)} %copy-done.1, bf16[4,32,32,256]{3,2,0,1:T(8,128)(2,1)} %collective-permute-done, bf16[160]{0:T(256)(128)(2,1)S(1)} %pad.113.clone), kind=kLoop, calls=%fused_computation.152 | loop fusion | flops 31457280 | bytes 18874688 | tf_op jit(solution)/shard_map/concatenate | solution.py:100
  103.0 20.2 %dynamic_update_slice.13 = bf16[4,32,160,256]{3,2,0,1:T(8,128)(2,1)} dynamic-update-slice(bf16[4,32,160,256]{3,2,0,1:T(8,128)(2,1)} %maximum_maximum_fusion, bf16[4,32,32,256]{3,2,0,1:T(8,128)(2,1)} %collective-permute-done.1, s32[]{:T(128)} %constant.279.clone.1, s32[]{:T(128)} %constant.279.clone.1, s32[]{:T(128)S(6)} %select_n.37, s32[]{:T(128)} %constant.279.clone.1) | dynamic-update-slice | bytes 4194308 | tf_op jit(solution)/shard_map/dynamic_update_slice | solution.py:101
  123.2 3.4 broadcast_in_dim.105
  126.6 53.5 %while.31 = (s32[]{:T(128)}, bf16[4,32,96,256]{3,2,0,1:T(8,128)(2,1)}, f32[96,256]{1,0:T(8,128)S(1)}, bf16[32,4,256,256]{3,2,1,0:T(8,128)(2,1)}, bf16[4,32,160,2...) while((s32[]{:T(128)}, ...), condition=%wide.region_1.0_spmd.clone, body=%wide.region_0.0_spmd.clone.sunk | while | flops 1311866880 | bytes 7342295 | solution.py:149
  126.6 1.7 constant_dynamic-slice_fusion.11
  128.4 4.9 fusion.136
  133.3 1.7 constant_dynamic-slice_fusion.11
  135.1 4.9 fusion.136
  139.9 1.7 constant_dynamic-slice_fusion.11
  141.7 4.9 fusion.136
  146.6 1.7 constant_dynamic-slice_fusion.11
  148.4 5.0 fusion.136
  153.4 1.7 constant_dynamic-slice_fusion.11
  155.1 4.9 fusion.136
  160.0 1.7 constant_dynamic-slice_fusion.11
  161.8 4.9 fusion.136
  166.7 1.7 constant_dynamic-slice_fusion.11
  168.5 4.9 fusion.136
  173.4 1.7 constant_dynamic-slice_fusion.11
  175.2 4.9 fusion.136
  180.1 5.5 %fusion.120 = (bf16[4,32,32,256]{3,2,0,1:T(8,128)(2,1)}, bf16[4,32,32,256]{3,2,0,1:T(8,128)(2,1)}) fusion(bf16[4,32,96,256]{3,2,0,1:T(8,128)(2,1)} %get-tuple-element.364, s32[]{:T(128)S(6)} %select_n.36), kind=kLoop, calls=%fused_computation.217 | loop fusion | bytes 8388612 | tf_op jit(solution)/shard_map/slice | solution.py:153
  185.6 22.0 %collective-permute-start.2 = (bf16[4,32,32,256]{3,2,0,1:T(8,128)(2,1)}, bf16[4,32,32,256]{3,2,0,1:T(8,128)(2,1)}, u32[]{:S(2)}, u32[]{:S(2)}) collective-permute-start(bf16[4,32,32,256]{3,2,0,1:T(8,128)(2,1)} %get-tuple-element.567), channel_id=1, source_target_pairs={{0,1},{1,2},{2,3},{3,4},{4,5},{5,6},{6,7},{7,8},{8,9},{9,10},{10,1... | collective-permute-start | bytes 6291464 | tf_op jit(solution)/shard_map/ppermute | solution.py:21
  209.0 2.1 reduce.2
  211.8 4.0 convert_bitcast_fusion.1
  215.7 8.3 %maximum_maximum_fusion.1 = bf16[4,32,160,256]{3,2,0,1:T(8,128)(2,1)} fusion(bf16[4,32,96,256]{3,2,0,1:T(8,128)(2,1)S(1)} %copy-done, bf16[4,32,32,256]{3,2,0,1:T(8,128)(2,1)} %collective-permute-done.2, bf16[160]{0:T(256)(128)(2,1)S(1)} %pad.113.clone), kind=kLoop, calls=%fused_computation.153 | loop fusion | flops 31457280 | bytes 18874688 | tf_op jit(solution)/shard_map/concatenate | solution.py:100
  224.0 20.2 %dynamic_update_slice.14 = bf16[4,32,160,256]{3,2,0,1:T(8,128)(2,1)} dynamic-update-slice(bf16[4,32,160,256]{3,2,0,1:T(8,128)(2,1)} %maximum_maximum_fusion.1, bf16[4,32,32,256]{3,2,0,1:T(8,128)(2,1)} %collective-permute-done.3, s32[]{:T(128)} %constant.279.clone.1, s32[]{:T(128)} %constant.279.clone.1, s32[]{:T(128)S(6)} %select_n.37, s32[]{:T(128)} %constant.279.clone.1) | dynamic-update-slice | bytes 4194308 | tf_op jit(solution)/shard_map/dynamic_update_slice | solution.py:101
  244.2 134.8 %while.32 = (s32[]{:T(128)}, f32[9,96,256]{2,1,0:T(8,128)S(1)}, f32[9,96,256]{2,1,0:T(8,128)S(1)}, f32[32]{0:T(128)S(1)}, bf16[32,4,256,256]{3,2,1,0:T(8,128)(2,...) while((s32[]{:T(128)}, f32[9,96,256]{2,1,0:T(8,128)S(1)}, ...), condition=%wide.region_21.22_spmd.clone, body=%wide.region_2.21_spmd.clone.sunk | while | flops 1872642304 | bytes 34342920 | solution.py:176
  244.2 2.5 constant_dynamic-slice_fusion.12
  247.4 4.9 fusion.140
  257.4 1.5 fusion.142
  261.0 2.5 constant_dynamic-slice_fusion.12
  264.2 4.9 fusion.140
  274.3 1.5 fusion.142
  277.9 2.5 constant_dynamic-slice_fusion.12
  281.1 4.9 fusion.140
  291.1 1.5 fusion.142
  294.7 2.5 constant_dynamic-slice_fusion.12
  297.9 4.9 fusion.140
  308.0 1.5 fusion.142
  311.6 2.5 constant_dynamic-slice_fusion.12
  314.8 4.9 fusion.140
  324.8 1.5 fusion.142
  328.4 2.5 constant_dynamic-slice_fusion.12
  331.6 4.9 fusion.140
  341.7 1.5 fusion.142
  345.3 2.5 constant_dynamic-slice_fusion.12
  348.5 4.9 fusion.140
  358.5 1.5 fusion.142
  362.2 2.5 constant_dynamic-slice_fusion.12
  365.3 4.9 fusion.140
  375.4 1.5 fusion.142
  379.0 1.8 all_gather_reshape.4
  380.8 119.5 %all-gather.2.cloned.1.call-done = f32[8,9,1,24576]{3,2,1,0:T(1,128)} async-done(((f32[1,9,1,24576]{3,2,1,0:T(1,128)}), f32[8,9,1,24576]{3,2,1,0:T(1,128)}) %all-gather.2.cloned.1.call-update) | async-done | bytes 7077904 | tf_op jit(solution)/shard_map/all_gather | solution.py:13
  500.3 19.7 %reduce_sum.423 = f32[9,24576]{1,0:T(8,128)S(1)} reduce(f32[8,9,1,24576]{3,2,1,0:T(1,128)} %all-gather.2.cloned.1.call-done, f32[]{:T(128)} %constant.280.clone.1), dimensions={0,2}, to_apply=%region_22.23 | reduce | flops 1548288 | bytes 7962628 | tf_op jit(solution)/shard_map/reduce_sum | solution.py:14
  (162 shorter events, 67.3 us)
Async XLA Ops:
  6.5 493.8 %all-gather.2.cloned.1.call-start = ((), (), s32[]{:S(2)}) async-start(), calls=%async_computation | async-start | bytes 7962624 | tf_op jit(solution)/shard_map/all_gather | solution.py:13
  56.1 3.9 copy-start.1
  56.1 8.0 %copy-start.4 = (bf16[32,4,65]{2,1,0:T(4,128)(2,1)S(1)}, bf16[32,4,65]{2,1,0:T(4,128)(2,1)}, u32[]{:S(2)}) copy-start(bf16[32,4,65]{2,1,0:T(4,128)(2,1)} %param.14) | copy-start | bytes 49924
  60.0 32.9 %collective-permute-start = (bf16[4,32,32,256]{3,2,0,1:T(8,128)(2,1)}, bf16[4,32,32,256]{3,2,0,1:T(8,128)(2,1)}, u32[]{:S(2)}, u32[]{:S(2)}) collective-permute-start(bf16[4,32,32,256]{3,2,0,1:T(8,128)(2,1)} %get-tuple-element.569), channel_id=1, source_target_pairs={{0,1},{1,2},{2,3},{3,4},{4,5},{5,6},{6,7},{7,8},{8,9},{9,10},{10,1... | collective-permute-start | bytes 6291464 | tf_op jit(solution)/shard_map/ppermute | solution.py:21
  62.7 40.4 %collective-permute-start.1 = (bf16[4,32,32,256]{3,2,0,1:T(8,128)(2,1)}, bf16[4,32,32,256]{3,2,0,1:T(8,128)(2,1)}, u32[]{:S(2)}, u32[]{:S(2)}) collective-permute-start(bf16[4,32,32,256]{3,2,0,1:T(8,128)(2,1)} %get-tuple-element.568), channel_id=1, source_target_pairs={{1,0},{2,1},{3,2},{4,3},{5,4},{6,5},{7,6},{8,7},{9,8},{10,9},{11,1... | collective-permute-start | bytes 6291464 | tf_op jit(solution)/shard_map/ppermute | solution.py:21
  72.6 16.4 %copy-start.3 = (s32[96,256]{1,0:T(8,128)S(1)}, s32[96,256]{1,0:T(8,128)}, u32[]{:S(2)}) copy-start(s32[96,256]{1,0:T(8,128)} %param.15) | copy-start | bytes 294916
  72.6 16.4 %copy-start.2 = (bf16[32,4,65]{2,1,0:T(4,128)(2,1)S(1)}, bf16[32,4,65]{2,1,0:T(4,128)(2,1)}, u32[]{:S(2)}) copy-start(bf16[32,4,65]{2,1,0:T(4,128)(2,1)} %param.13) | copy-start | bytes 49924
  123.2 3.4 copy-start.5
  185.6 30.1 %collective-permute-start.2 = (bf16[4,32,32,256]{3,2,0,1:T(8,128)(2,1)}, bf16[4,32,32,256]{3,2,0,1:T(8,128)(2,1)}, u32[]{:S(2)}, u32[]{:S(2)}) collective-permute-start(bf16[4,32,32,256]{3,2,0,1:T(8,128)(2,1)} %get-tuple-element.567), channel_id=1, source_target_pairs={{0,1},{1,2},{2,3},{3,4},{4,5},{5,6},{6,7},{7,8},{8,9},{9,10},{10,1... | collective-permute-start | bytes 6291464 | tf_op jit(solution)/shard_map/ppermute | solution.py:21
  207.6 16.4 %collective-permute-start.3 = (bf16[4,32,32,256]{3,2,0,1:T(8,128)(2,1)}, bf16[4,32,32,256]{3,2,0,1:T(8,128)(2,1)}, u32[]{:S(2)}, u32[]{:S(2)}) collective-permute-start(bf16[4,32,32,256]{3,2,0,1:T(8,128)(2,1)} %get-tuple-element.566), channel_id=1, source_target_pairs={{1,0},{2,1},{3,2},{4,3},{5,4},{6,5},{7,6},{8,7},{9,8},{10,9},{11,1... | collective-permute-start | bytes 6291464 | tf_op jit(solution)/shard_map/ppermute | solution.py:21
  211.7 4.0 copy-start
Sparse Core Ops, SparseCore 0:
  380.9 119.3 all-gather.1
